TPU v7x, 512 devices: a whole 4x8x8 slice. The times are simulated.
512 devices in a mesh: dp: 128 (over y, z, core), tp: 4 (over x).
Axes of the slice: x: 4, y: 8, z: 8, core: 2. Of those that a mesh axis runs over, the one named last changes fastest.
Arguments:
- hidden: bfloat16 [2048, 2048], P('dp'), may hold values from -6 to 6
- routes: int32 [2048, 8], P('dp'), may hold values from 0 to 127, all different within a row; in each aligned block of 16 rows (0 to 15, 16 to 31, ...) at most 2 rows name the same one
- route_weights: int32 [2048, 8], P('dp'), may hold values from 1 to 65535
- w_gate: bfloat16 [128, 2048, 1024], P('dp', None, 'tp'), may hold values from -0.125 to 0.125
- w_up: bfloat16 [128, 2048, 1024], P('dp', None, 'tp'), may hold values from -0.125 to 0.125
- w_down: bfloat16 [128, 1024, 2048], P('dp', 'tp'), may hold values from -0.1875 to 0.1875
- queries: bfloat16 [1024, 8192], P('dp', 'tp'), may hold values from -480 to 480
- key_codes: bfloat16 [262144, 512], P('dp', 'tp'), may hold values from -127 to 127, as said below
- key_scales: float32 [4, 262144], P('tp', 'dp'), may hold values from 0.004 to 0.02
- cache_values: bfloat16 [262144, 512], P('dp', 'tp'), may hold values from -6 to 6
- new_keys: bfloat16 [1024, 512], P('dp', 'tp'), may hold values from -6 to 6
- new_values: bfloat16 [1024, 512], P('dp', 'tp'), may hold values from -6 to 6
- lengths: int32 [1024], P('dp'), may hold values from 1 to 2041, as said below
Outputs:
- expert_mix: bfloat16 [2048, 2048], P('dp')
- attended: bfloat16 [1024, 8192], P('dp', 'tp')
Inputs may be any that keep to these rules, and one draw needn't show every extreme that they name: `lengths`: the 8 requests of each block sum to at most 2048 positions; in every draw some block sums to exactly 2048, one of its requests holding 2048 - 7 positions. `routes`: each row names 8 different experts. Among the rows of one index of dp no expert is named more than 2 times, and in every draw some expert is named exactly 2 times by the rows of some index. `key_codes`: whole numbers.
All inputs are finite; a program needn't handle non-finite values.
Results may differ from a plain program's by a relative error of at most 0.014.
The roundings to bfloat16 on the way count: a program that leaves them out, or rounds other values in their place, can miss the bound.
Values may be sent and summed in bfloat16 or wider, within the bound.
No kernel may reach another device: no remote copies, remote signals or barrier semaphores. Data moves between devices by JAX's collectives and lax.ppermute only.
A program may use at most 64 MiB of HBM per device.

v0:
```python
import jax
import jax.numpy as jnp
from jax import lax
from jax.sharding import PartitionSpec as P

rope_base = 1000000.0


def inverse_freq(head_size):
    steps = jnp.arange(head_size // 2, dtype=jnp.float32) * (2.0 / head_size)
    return jnp.exp(-steps * jnp.log(jnp.float32(rope_base)))


def rotate(vector, angles):
    half_size = vector.shape[-1] // 2
    front_half = vector[..., :half_size]
    back_half = vector[..., half_size:]
    cosine = jnp.cos(angles)
    sine_part = jnp.sin(angles)
    return jnp.concatenate(
        [front_half * cosine - back_half * sine_part, back_half * cosine + front_half * sine_part],
        axis=-1,
    )


def attend_local(queries, codes, scales, cache_values, new_keys, new_values, lengths):
    row_count = queries.shape[0]
    cache_len = codes.shape[0]
    groups = scales.shape[0]
    head_size = codes.shape[1] // groups
    per_group = queries.shape[1] // (groups * head_size)
    request_end = jnp.cumsum(lengths)
    starts = request_end - lengths
    cache_pos = jnp.arange(cache_len, dtype=jnp.int32)
    member = (cache_pos[:, None] >= starts[None, :]) & (cache_pos[:, None] < request_end[None, :])
    offset = jnp.sum(jnp.where(member, starts[None, :], 0), axis=1)
    position = (cache_pos - offset).astype(jnp.float32)
    frequency = inverse_freq(head_size)
    cache_keys = (
        codes.astype(jnp.float32).reshape(cache_len, groups, head_size)
        * jnp.transpose(scales)[:, :, None]
    )
    cache_keys = rotate(cache_keys, position[:, None, None] * frequency[None, None, :]).astype(
        jnp.bfloat16
    )
    query_angles = lengths.astype(jnp.float32)[:, None] * frequency[None, :]
    rotated_query = queries.astype(jnp.float32).reshape(row_count, groups, per_group, head_size)
    rotated_query = rotate(rotated_query, query_angles[:, None, None, :]).astype(jnp.bfloat16)
    fresh_key = rotate(
        new_keys.astype(jnp.float32).reshape(row_count, groups, head_size), query_angles[:, None, :]
    ).astype(jnp.bfloat16)
    score_scale = head_size ** (-0.5)
    scores = (
        jnp.einsum("rgqd,cgd->rgqc", rotated_query, cache_keys, preferred_element_type=jnp.float32)
        * score_scale
    )
    own_score = (
        jnp.einsum("rgqd,rgd->rgq", rotated_query, fresh_key, preferred_element_type=jnp.float32)
        * score_scale
    )
    live_mask = jnp.transpose(member)[:, None, None, :]
    scores = jnp.where(live_mask, scores, -jnp.inf)
    peak_score = jnp.maximum(jnp.max(scores, axis=-1), own_score)
    weights = jnp.exp(scores - peak_score[..., None])
    own_weight = jnp.exp(own_score - peak_score)
    weight_sum = jnp.sum(weights, axis=-1) + own_weight
    value_rows = cache_values.reshape(cache_len, groups, head_size)
    mixture = jnp.einsum(
        "rgqc,cgd->rgqd",
        weights.astype(jnp.bfloat16),
        value_rows,
        preferred_element_type=jnp.float32,
    )
    mixture = mixture + own_weight[..., None] * new_values.astype(jnp.float32).reshape(
        row_count, groups, 1, head_size
    )
    return (
        (mixture / weight_sum[..., None])
        .reshape(row_count, groups * per_group * head_size)
        .astype(jnp.bfloat16)
    )


def expert_block(arrived, w_gate, w_up, w_down):
    arrived_shape = arrived.shape
    inputs = arrived.reshape(-1, arrived_shape[-1])
    gate_act = jnp.dot(inputs, w_gate[0], preferred_element_type=jnp.float32)
    up_act = jnp.dot(inputs, w_up[0], preferred_element_type=jnp.float32)
    hidden_act = (jax.nn.silu(gate_act) * up_act).astype(jnp.bfloat16)
    partial_value = jnp.dot(hidden_act, w_down[0], preferred_element_type=jnp.float32)
    return partial_value.reshape(arrived_shape[0], arrived_shape[1], partial_value.shape[-1])


def on_device(
    hidden,
    routes,
    route_weights,
    w_gate,
    w_up,
    w_down,
    queries,
    key_codes,
    key_scales,
    cache_values,
    new_keys,
    new_values,
    lengths,
):
    token_count = routes.shape[0]
    top_count = routes.shape[1]
    model_width = hidden.shape[1]
    tp_size = lax.axis_size("tp")
    dp_size = lax.axis_size("dp")
    slice_width = model_width // tp_size
    experts = dp_size * w_gate.shape[0]
    capacity = min(token_count, max(2, token_count * top_count * 2 // experts))
    flat_ids = routes.reshape(-1)
    onehot = (flat_ids[:, None] == jnp.arange(experts, dtype=jnp.int32)[None, :]).astype(jnp.int32)
    rank_ids = jnp.sum(onehot * (jnp.cumsum(onehot, axis=0) - 1), axis=1)
    slot_ids = flat_ids * capacity + rank_ids
    slot_grid = slot_ids.reshape(token_count, top_count)
    selector = jnp.any(
        jnp.arange(experts * capacity, dtype=jnp.int32)[:, None, None] == slot_grid[None, :, :],
        axis=2,
    ).astype(jnp.bfloat16)
    tp_index = lax.axis_index("tp")
    own_cols = lax.dynamic_slice_in_dim(hidden, tp_index * slice_width, slice_width, axis=1)
    outgoing = jnp.dot(selector, own_cols, preferred_element_type=jnp.float32).astype(jnp.bfloat16)
    outgoing = outgoing.reshape(experts, capacity, slice_width)
    arrived = lax.all_to_all(outgoing, "dp", split_axis=0, concat_axis=0, tiled=True)
    arrived = lax.all_gather(arrived, "tp", axis=0, tiled=False)
    slots = dp_size * capacity
    arrived = arrived.reshape(tp_size, slots, slice_width)
    gate_w = w_gate[0].reshape(tp_size, slice_width, w_gate.shape[2])
    up_w = w_up[0].reshape(tp_size, slice_width, w_up.shape[2])
    gate_act = jnp.einsum("tsd,tdh->sh", arrived, gate_w, preferred_element_type=jnp.float32)
    up_act = jnp.einsum("tsd,tdh->sh", arrived, up_w, preferred_element_type=jnp.float32)
    hidden_act = (jax.nn.silu(gate_act) * up_act).astype(jnp.bfloat16)
    partial_value = jnp.dot(hidden_act, w_down[0], preferred_element_type=jnp.float32)
    partial_value = partial_value.astype(jnp.bfloat16).reshape(slots, tp_size, slice_width)
    gathered = lax.all_to_all(partial_value, "tp", split_axis=1, concat_axis=1, tiled=True)
    expert_out = jnp.sum(gathered.astype(jnp.float32), axis=1).astype(jnp.bfloat16)
    expert_out = expert_out.reshape(dp_size, capacity, slice_width)
    returned = lax.all_to_all(expert_out, "dp", split_axis=0, concat_axis=0, tiled=True)
    picked = jnp.take(returned.reshape(experts * capacity, slice_width), slot_ids, axis=0)
    picked = picked.reshape(token_count, top_count, slice_width)
    shares = route_weights.astype(jnp.float32)
    shares = shares / jnp.sum(shares, axis=1, keepdims=True)
    mix_cols = jnp.einsum("tk,tkd->td", shares, picked.astype(jnp.float32)).astype(jnp.bfloat16)
    expert_mix = lax.all_gather(mix_cols, "tp", axis=1, tiled=True)
    attended = attend_local(
        queries, key_codes, key_scales, cache_values, new_keys, new_values, lengths
    )
    return (expert_mix, attended)


def solution(mesh):
    placed = (
        P("dp", None),
        P("dp", None),
        P("dp", None),
        P("dp", None, "tp"),
        P("dp", None, "tp"),
        P("dp", "tp", None),
        P("dp", "tp"),
        P("dp", "tp"),
        P("tp", "dp"),
        P("dp", "tp"),
        P("dp", "tp"),
        P("dp", "tp"),
        P("dp"),
    )
    return jax.shard_map(
        on_device,
        mesh=mesh,
        in_specs=placed,
        out_specs=(P("dp", None), P("dp", "tp")),
        check_vma=False,
    )
```

profile of v0, /device:TPU:8, one launch (start us, length us, event | category | flops | bytes accessed | tf_op | source)
XLA Modules:
  0.0 142.3 jit_solution(14156088460898718591)
XLA Ops:
  7.2 0.8 copy.22
  8.3 0.2 reduce_window_sum.18
  8.4 0.2 select_reduce_fusion.1
  8.7 0.1 fusion.34
  8.9 1.0 convolution_convert_fusion.1
  9.9 0.8 reshape.483
  10.7 17.4 %all-to-all-start = ((bf16[128,2,512]{2,1,0:T(2,128)(2,1)}), bf16[128,2,512]{2,1,0:T(2,128)(2,1)S(1)}, u32[]{:S(2)}, u32[]{:S(2)}) async-start(bf16[128,2,512]{2,1,0:T(2,128)(2,1)} %reshape.483), calls=%async_computation | async-start | bytes 524288 | tf_op jit(solution)/shard_map/all_to_all | solution.py:130
  28.2 0.2 reduce-window.8
  29.1 13.7 %all-to-all-done = bf16[128,2,512]{2,1,0:T(2,128)(2,1)S(1)} async-done(((bf16[128,2,512]{2,1,0:T(2,128)(2,1)}), bf16[128,2,512]{2,1,0:T(2,128)(2,1)S(1)}, u32[]{:S(2)}, u32[]{:S(2)}) %all-to-all-start) | async-done | bytes 262176 | tf_op jit(solution)/shard_map/all_to_all | solution.py:130
  42.8 0.7 copy-done.1
  43.7 0.3 multiply_bitcast_fusion
  44.1 4.8 %fusion.26 = (bf16[2048,64]{1,0:T(8,128)(2,1)S(1)}, bf16[2048,64]{1,0:T(8,128)(2,1)S(1)}) fusion(f32[2048,1,128]{2,0,1:T(8,128)S(1)} %multiply_bitcast_fusion, f32[64]{0:T(128)S(1)} %multiply_exponential_fusion, f32[2048]{0:T(1024)S(1)} %subtract_convert_fusion.1), kind=kLoop, calls=%fused_computation.38 | loop fusion | flops 1179648 | bytes 1581312 | tf_op jit(solution)/shard_map/concatenate | solution.py:20
  48.9 0.5 fusion.65
  49.4 16.5 %all-gather.3.cloned.1.call-done = bf16[512,2,512]{2,1,0:T(2,128)(2,1)} async-done(((bf16[128,2,512]{2,1,0:T(2,128)(2,1)}), bf16[512,2,512]{2,1,0:T(2,128)(2,1)}) %all-gather.3.cloned.1.call-update) | async-done | bytes 1048592 | tf_op jit(solution)/shard_map/all_gather | solution.py:131
  65.9 1.5 %reshape.484 = bf16[4,256,512]{2,1,0:T(8,128)(2,1)S(1)} reshape(bf16[512,2,512]{2,1,0:T(2,128)(2,1)} %all-gather.3.cloned.1.call-done) | data formatting | bytes 2097152 | tf_op jit(solution)/shard_map/reshape | solution.py:133
  67.4 1.7 %convolution_bitcast_fusion.1 = f32[256,256]{1,0:T(8,128)S(1)} fusion(bf16[4,256,512]{2,1,0:T(8,128)(2,1)S(1)} %reshape.484, bf16[4,512,256]{2,1,0:T(8,128)(2,1)} %bitcast.111), kind=kOutput, calls=%fused_computation.14 | convolution fusion | flops 268435456 | bytes 2359296 | tf_op jit(solution)/shard_map/tsd,tdh->sh/dot_general | solution.py:136
  69.1 3.5 %convolution_convert_fusion = bf16[256,2048]{1,0:T(8,128)(2,1)} fusion(bf16[4,256,512]{2,1,0:T(8,128)(2,1)S(1)} %reshape.484, bf16[4,512,256]{2,1,0:T(8,128)(2,1)S(1)} %bitcast.109, bf16[1,256,2048]{2,1,0:T(8,128)(2,1)} %param.18, f32[256,256]{1,0:T(8,128)S(1)} %convolution_bitcast_fusion.1), kind=kOutput, calls=%fused_computation.1 | convolution fusion | flops 537788416 | bytes 4456448 | tf_op jit(solution)/shard_map/dot_general | solution.py:139
  72.6 2.4 %copy.38 = bf16[32,4,8,512]{3,2,0,1:T(8,128)(2,1)} copy(bf16[32,4,8,512]{3,2,1,0:T(8,128)(2,1)} %bitcast.112) | data formatting | bytes 2097152 | tf_op jit(solution)/shard_map/reshape | solution.py:140
  74.9 3.5 %all-to-all-start.1 = ((bf16[256,4,512]{2,0,1:T(8,128)(2,1)}), bf16[256,4,512]{2,0,1:T(8,128)(2,1)S(1)}, u32[]{:S(2)}, u32[]{:S(2)}) async-start(bf16[256,4,512]{2,0,1:T(8,128)(2,1)} %bitcast.110), calls=%async_computation.1 | async-start | bytes 2097152 | tf_op jit(solution)/shard_map/all_to_all | solution.py:141
  78.5 0.2 fusion.47
  78.7 0.3 fusion.17
  79.0 12.9 %all-to-all-done.1 = bf16[256,4,512]{2,0,1:T(8,128)(2,1)S(1)} async-done(((bf16[256,4,512]{2,0,1:T(8,128)(2,1)}), bf16[256,4,512]{2,0,1:T(8,128)(2,1)S(1)}, u32[]{:S(2)}, u32[]{:S(2)}) %all-to-all-start.1) | async-done | bytes 1048608 | tf_op jit(solution)/shard_map/all_to_all | solution.py:141
  91.8 0.2 reduce_sum.55
  92.1 0.8 reshape.486
  92.9 14.2 %all-to-all-start.2 = ((bf16[128,2,512]{2,1,0:T(2,128)(2,1)}), bf16[128,2,512]{2,1,0:T(2,128)(2,1)S(1)}, u32[]{:S(2)}, u32[]{:S(2)}) async-start(bf16[128,2,512]{2,1,0:T(2,128)(2,1)} %reshape.486), calls=%async_computation.2 | async-start | bytes 524288 | tf_op jit(solution)/shard_map/all_to_all | solution.py:144
  107.1 0.4 fusion.11
  107.4 0.6 copy.40
  108.1 13.7 %all-to-all-done.2 = bf16[128,2,512]{2,1,0:T(2,128)(2,1)S(1)} async-done(((bf16[128,2,512]{2,1,0:T(2,128)(2,1)}), bf16[128,2,512]{2,1,0:T(2,128)(2,1)S(1)}, u32[]{:S(2)}, u32[]{:S(2)}) %all-to-all-start.2) | async-done | bytes 262176 | tf_op jit(solution)/shard_map/all_to_all | solution.py:144
  121.9 0.8 gather_fusion
  122.7 0.2 fusion.32
  123.0 11.9 %all_gather.11 = bf16[16,2048]{1,0:T(8,128)(2,1)S(1)} all-gather(bf16[16,512]{1,0:T(8,128)(2,1)S(1)} %bitcast.114), channel_id=1, replica_groups=mesh['dp'=128,'tp'=4] {'tp'}, dimensions={1}, use_global_device_ids=true | all-gather | bytes 81920 | tf_op jit(solution)/shard_map/all_gather | solution.py:150
  134.9 0.6 copy.43
  (49 shorter events, 1.4 us)
Async XLA Ops:
  7.2 61.9 %copy-start = (bf16[1,2048,256]{2,1,0:T(8,128)(2,1)S(1)}, bf16[1,2048,256]{2,1,0:T(8,128)(2,1)}, u32[]{:S(2)}) copy-start(bf16[1,2048,256]{2,1,0:T(8,128)(2,1)} %param.17) | copy-start | bytes 3145732
  7.2 21.0 %copy-start.5 = (s32[16,8]{0,1:T(8,128)S(1)}, s32[16,8]{0,1:T(8,128)}, u32[]{:S(2)}) copy-start(s32[16,8]{0,1:T(8,128)} %param.15) | copy-start | bytes 1540
  7.2 21.0 %copy-start.4 = (bf16[8,2048]{1,0:T(8,128)(2,1)S(1)}, bf16[8,2048]{1,0:T(8,128)(2,1)}, u32[]{:S(2)}) copy-start(bf16[8,2048]{1,0:T(8,128)(2,1)} %param.19) | copy-start | bytes 98308
  7.2 21.0 %copy-start.9 = (s32[8]{0:T(128)S(1)}, s32[8]{0:T(128)}, u32[]{:S(2)}) copy-start(s32[8]{0:T(128)} %param.25) | copy-start | bytes 100
  7.2 21.3 %copy-start.7 = (bf16[8,128]{1,0:T(8,128)(2,1)S(1)}, bf16[8,128]{1,0:T(8,128)(2,1)}, u32[]{:S(2)}) copy-start(bf16[8,128]{1,0:T(8,128)(2,1)} %param.23) | copy-start | bytes 6148
  7.2 21.8 %copy-start.8 = (bf16[8,128]{1,0:T(8,128)(2,1)S(1)}, bf16[8,128]{1,0:T(8,128)(2,1)}, u32[]{:S(2)}) copy-start(bf16[8,128]{1,0:T(8,128)(2,1)} %param.24) | copy-start | bytes 6148
  8.8 34.9 %copy-start.2 = (bf16[2048,128]{1,0:T(8,128)(2,1)S(1)}, bf16[2048,128]{1,0:T(8,128)(2,1)}, u32[]{:S(2)}) copy-start(bf16[2048,128]{1,0:T(8,128)(2,1)} %param.20) | copy-start | bytes 1572868
  8.9 34.9 %copy-start.6 = (f32[1,2048]{1,0:T(1,128)S(1)}, f32[1,2048]{1,0:T(1,128)}, u32[]{:S(2)}) copy-start(f32[1,2048]{1,0:T(1,128)} %param.21) | copy-start | bytes 24580
  10.7 32.1 %all-to-all-start = ((bf16[128,2,512]{2,1,0:T(2,128)(2,1)}), bf16[128,2,512]{2,1,0:T(2,128)(2,1)S(1)}, u32[]{:S(2)}, u32[]{:S(2)}) async-start(bf16[128,2,512]{2,1,0:T(2,128)(2,1)} %reshape.483), calls=%async_computation | async-start | bytes 524288 | tf_op jit(solution)/shard_map/all_to_all | solution.py:130
  28.1 37.8 %all-gather.3.cloned.1.call-start = ((), (), s32[]{:S(2)}) async-start(), calls=%async_computation.3 | async-start | bytes 1310720 | tf_op jit(solution)/shard_map/all_gather | solution.py:131
  42.8 0.7 copy-start.1
  74.9 16.9 %all-to-all-start.1 = ((bf16[256,4,512]{2,0,1:T(8,128)(2,1)}), bf16[256,4,512]{2,0,1:T(8,128)(2,1)S(1)}, u32[]{:S(2)}, u32[]{:S(2)}) async-start(bf16[256,4,512]{2,0,1:T(8,128)(2,1)} %bitcast.110), calls=%async_computation.1 | async-start | bytes 2097152 | tf_op jit(solution)/shard_map/all_to_all | solution.py:141
  92.1 15.0 %copy-start.3 = (bf16[2048,128]{1,0:T(8,128)(2,1)S(1)}, bf16[2048,128]{1,0:T(8,128)(2,1)}, u32[]{:S(2)}) copy-start(bf16[2048,128]{1,0:T(8,128)(2,1)} %param.22) | copy-start | bytes 1572868
  92.9 28.9 %all-to-all-start.2 = ((bf16[128,2,512]{2,1,0:T(2,128)(2,1)}), bf16[128,2,512]{2,1,0:T(2,128)(2,1)S(1)}, u32[]{:S(2)}, u32[]{:S(2)}) async-start(bf16[128,2,512]{2,1,0:T(2,128)(2,1)} %reshape.486), calls=%async_computation.2 | async-start | bytes 524288 | tf_op jit(solution)/shard_map/all_to_all | solution.py:144
Sparse Core Ops, SparseCore 0:
  43.7 22.2 all-gather.2
where the time goes:
time: 143 us; the launch traced here: 142 us
  waiting for transfers between devices  56.8 us (40%)
  starting transfers between devices  35.1 us (25%)
  between operations  14.4 us (10%)
  blocking collectives  11.9 us (8%)
  local copies, waits for them, and re-layouts  9.56 us (7%)
  matrix products  7.53 us (5%)
  other arithmetic  7.1 us (5%)
    all_to_all x1, starting transfers between devices, on_device(): lax.all_to_all(outgoing, 'dp', split_axis=0, concat_axis=0, tiled=True)  17.4 us
    all_gather x1, waiting for transfers between devices, on_device(): arrived = lax.all_gather(arrived, 'tp', axis=0, tiled=False)  16.5 us
    all_to_all x1, starting transfers between devices, on_device(): lax.all_to_all(expert_out, 'dp', split_axis=0, concat_axis=0, tiled=True)  14.2 us
    all_to_all x1, waiting for transfers between devices, on_device(): lax.all_to_all(outgoing, 'dp', split_axis=0, concat_axis=0, tiled=True)  13.7 us
    all_to_all x1, waiting for transfers between devices, on_device(): lax.all_to_all(expert_out, 'dp', split_axis=0, concat_axis=0, tiled=True)  13.7 us
    all_to_all x1, waiting for transfers between devices, on_device(): lax.all_to_all(partial_value, 'tp', split_axis=1, concat_axis=1, tiled=True)  12.9 us
    all_gather x1, blocking collectives, on_device(): expert_mix = lax.all_gather(mix_cols, 'tp', axis=1, tiled=True)  11.9 us
    concatenate x4, other arithmetic, rotate(): jnp.concatenate([front_half * cosine - back_half * sine_part, back_half *...  5.09 us
  transfers between devices with their start and end apart: 4, of which 4 were waited for; matrix products, arithmetic and copies ran while one was open for 6% of the time, Pallas kernels for 0%

commit v1 on v0

--- a/solution.py
+++ b/solution.py
@@ -1,9 +1,21 @@
+import functools
 import jax
 import jax.numpy as jnp
 from jax import lax
 from jax.sharding import PartitionSpec as P
 
 rope_base = 1000000.0
+
+
+def sizes_use(in_array, on_dim):
+    carry_in = jnp.concatenate(
+        lax.all_to_all(jnp.stack(tuple((in_array for _ in range(lax.psum(1, "tp"))))), "tp", 0, 0),
+        axis=on_dim,
+    )
+    return carry_in
+
+
+edit_the_core = functools.partial(sizes_use, on_dim=1)
 
 
 def inverse_freq(head_size):
@@ -147,7 +159,7 @@
     shares = route_weights.astype(jnp.float32)
     shares = shares / jnp.sum(shares, axis=1, keepdims=True)
     mix_cols = jnp.einsum("tk,tkd->td", shares, picked.astype(jnp.float32)).astype(jnp.bfloat16)
-    expert_mix = lax.all_gather(mix_cols, "tp", axis=1, tiled=True)
+    expert_mix = edit_the_core(mix_cols)
     attended = attend_local(
         queries, key_codes, key_scales, cache_values, new_keys, new_values, lengths
     )

time: 143 us -> 137 us (0.958)
  blocking collectives: 11.9 us -> 0 us
  waiting for transfers between devices: 56.8 us -> 60.4 us
  starting transfers between devices: 35.1 us -> 38.4 us
    all_gather x1 -> x0, blocking collectives: 11.9 us -> none  [on_device(): expert_mix = lax.all_gather(mix_cols, 'tp', axis=1, tiled=True)]
    all_to_all x0 -> x1, waiting for transfers between devices: none -> 4.59 us  [sizes_use(): lax.all_to_all(jnp.stack(tuple((in_array for _ in range(lax.psum(1, 'tp')...]
    all_to_all x0 -> x1, starting transfers between devices: none -> 3.28 us  [sizes_use(): lax.all_to_all(jnp.stack(tuple((in_array for _ in range(lax.psum(1, 'tp')...]
    all_to_all x1, waiting for transfers between devices: 12.9 us -> 11.3 us  [on_device(): lax.all_to_all(partial_value, 'tp', split_axis=1, concat_axis=1, tiled=True)]
  transfers between devices with their start and end apart: 4 -> 5, of which waited for: 4 -> 5; matrix products, arithmetic and copies ran while one was open for 6% -> 7% of each run, Pallas kernels for 0% -> 0%
where the time goes in v1:
time: 137 us; the launch traced here: 136 us
  waiting for transfers between devices  60.4 us (44%)
  starting transfers between devices  38.4 us (28%)
  between operations  14.4 us (11%)
  local copies, waits for them, and re-layouts  8.94 us (7%)
  other arithmetic  7.86 us (6%)
  matrix products  6.52 us (5%)
    all_to_all x1, starting transfers between devices, on_device(): lax.all_to_all(outgoing, 'dp', split_axis=0, concat_axis=0, tiled=True)  17.4 us
    all_gather x1, waiting for transfers between devices, on_device(): arrived = lax.all_gather(arrived, 'tp', axis=0, tiled=False)  16.3 us
    all_to_all x1, waiting for transfers between devices, on_device(): lax.all_to_all(expert_out, 'dp', split_axis=0, concat_axis=0, tiled=True)  14.3 us
    all_to_all x1, starting transfers between devices, on_device(): lax.all_to_all(expert_out, 'dp', split_axis=0, concat_axis=0, tiled=True)  14.2 us
    all_to_all x1, waiting for transfers between devices, on_device(): lax.all_to_all(outgoing, 'dp', split_axis=0, concat_axis=0, tiled=True)  13.8 us
    all_to_all x1, waiting for transfers between devices, on_device(): lax.all_to_all(partial_value, 'tp', split_axis=1, concat_axis=1, tiled=True)  11.3 us
    concatenate x4, other arithmetic, rotate(): jnp.concatenate([front_half * cosine - back_half * sine_part, back_half *...  5.86 us
    all_to_all x1, waiting for transfers between devices, sizes_use(): lax.all_to_all(jnp.stack(tuple((in_array for _ in range(lax.psum(1, 'tp')...  4.59 us
  transfers between devices with their start and end apart: 5, of which 5 were waited for; matrix products, arithmetic and copies ran while one was open for 7% of the time, Pallas kernels for 0%

profile of v1, /device:TPU:8, one launch (start us, length us, event | category | flops | bytes accessed | tf_op | source)
XLA Modules:
  0.0 136.5 jit_solution(10404138661684247856)
XLA Ops:
  7.2 0.8 copy.26
  8.2 0.2 reduce_window_sum.18
  8.9 1.0 convolution_convert_fusion.1
  9.9 0.8 reshape.491
  10.7 17.4 %all-to-all-start = ((bf16[128,2,512]{2,1,0:T(2,128)(2,1)}), bf16[128,2,512]{2,1,0:T(2,128)(2,1)S(1)}, u32[]{:S(2)}, u32[]{:S(2)}) async-start(bf16[128,2,512]{2,1,0:T(2,128)(2,1)} %reshape.491), calls=%async_computation | async-start | bytes 524288 | tf_op jit(solution)/shard_map/all_to_all | solution.py:142
  28.3 0.2 reduce-window.8
  29.0 13.8 %all-to-all-done = bf16[128,2,512]{2,1,0:T(2,128)(2,1)S(1)} async-done(((bf16[128,2,512]{2,1,0:T(2,128)(2,1)}), bf16[128,2,512]{2,1,0:T(2,128)(2,1)S(1)}, u32[]{:S(2)}, u32[]{:S(2)}) %all-to-all-start) | async-done | bytes 262176 | tf_op jit(solution)/shard_map/all_to_all | solution.py:142
  42.8 0.7 copy-done.2
  43.7 0.3 multiply_bitcast_fusion
  44.0 5.6 %fusion.26 = (bf16[2048,64]{1,0:T(8,128)(2,1)}, bf16[2048,64]{1,0:T(8,128)(2,1)}) fusion(f32[2048,1,128]{2,0,1:T(8,128)S(1)} %multiply_bitcast_fusion, f32[64]{0:T(128)S(1)} %multiply_exponential_fusion, f32[2048]{0:T(1024)S(1)} %subtract_convert_fusion.1), kind=kLoop, calls=%fused_computation.38 | loop fusion | flops 1179648 | bytes 1581312 | tf_op jit(solution)/shard_map/concatenate | solution.py:32
  49.6 16.3 %all-gather.3.cloned.1.call-done = bf16[512,2,512]{2,1,0:T(2,128)(2,1)} async-done(((bf16[128,2,512]{2,1,0:T(2,128)(2,1)}), bf16[512,2,512]{2,1,0:T(2,128)(2,1)}) %all-gather.3.cloned.1.call-update) | async-done | bytes 1048592 | tf_op jit(solution)/shard_map/all_gather | solution.py:143
  65.9 1.5 %reshape.492 = bf16[4,256,512]{2,1,0:T(8,128)(2,1)S(1)} reshape(bf16[512,2,512]{2,1,0:T(2,128)(2,1)} %all-gather.3.cloned.1.call-done) | data formatting | bytes 2097152 | tf_op jit(solution)/shard_map/reshape | solution.py:145
  67.4 0.4 convolution_bitcast_fusion.1
  67.9 2.5 %convolution_convert_fusion = bf16[256,2048]{1,0:T(8,128)(2,1)S(1)} fusion(bf16[4,256,512]{2,1,0:T(8,128)(2,1)S(1)} %reshape.492, bf16[4,512,256]{2,1,0:T(8,128)(2,1)S(1)} %bitcast.112, bf16[1,256,2048]{2,1,0:T(8,128)(2,1)} %param.18, f32[256,256]{1,0:T(8,128)S(1)} %convolution_bitcast_fusion.1), kind=kOutput, calls=%fused_computation.1 | convolution fusion | flops 537788416 | bytes 4456448 | tf_op jit(solution)/shard_map/dot_general | solution.py:151
  70.4 1.1 copy.44
  71.4 3.5 %all-to-all-start.1 = ((bf16[256,4,512]{2,0,1:T(8,128)(2,1)}), bf16[256,4,512]{2,0,1:T(8,128)(2,1)S(1)}, u32[]{:S(2)}, u32[]{:S(2)}) async-start(bf16[256,4,512]{2,0,1:T(8,128)(2,1)} %bitcast.108), calls=%async_computation.1 | async-start | bytes 2097152 | tf_op jit(solution)/shard_map/all_to_all | solution.py:153
  75.0 0.2 fusion.47
  75.2 1.7 %fusion.65 = (f32[8,16]{1,0:T(8,128)S(1)}, f32[8,1,16,2048]{3,2,0,1:T(8,128)S(1)}) fusion(bf16[8,16,64]{2,1,0:T(8,128)(2,1)S(1)} %get-tuple-element.9, bf16[8,16,64]{2,1,0:T(8,128)(2,1)S(1)} %get-tuple-element.8, bf16[2048,64]{1,0:T(8,128)(2,1)} %get-tuple-element.7, bf16[2048,64]{1,0:T(8,128)(2,1)} %get-tuple-element.6, pred[8,2048]{1,0:T(8,128)(4,1)S(1)} %fusion.38), kind=kOutput, calls=%fused_computation.111 | convolution fusion | flops 69009280 | bytes 1622528 | tf_op jit(solution)/shard_map/rgqd,cgd->rgqc/dot_general | solution.py:66
  77.0 11.3 %all-to-all-done.1 = bf16[256,4,512]{2,0,1:T(8,128)(2,1)S(1)} async-done(((bf16[256,4,512]{2,0,1:T(8,128)(2,1)}), bf16[256,4,512]{2,0,1:T(8,128)(2,1)S(1)}, u32[]{:S(2)}, u32[]{:S(2)}) %all-to-all-start.1) | async-done | bytes 1048608 | tf_op jit(solution)/shard_map/all_to_all | solution.py:153
  88.3 0.2 reduce_sum.55
  88.6 0.8 reshape.494
  89.4 14.2 %all-to-all-start.2 = ((bf16[128,2,512]{2,1,0:T(2,128)(2,1)}), bf16[128,2,512]{2,1,0:T(2,128)(2,1)S(1)}, u32[]{:S(2)}, u32[]{:S(2)}) async-start(bf16[128,2,512]{2,1,0:T(2,128)(2,1)} %reshape.494), calls=%async_computation.2 | async-start | bytes 524288 | tf_op jit(solution)/shard_map/all_to_all | solution.py:156
  103.7 0.3 fusion.17
  104.0 14.3 %all-to-all-done.2 = bf16[128,2,512]{2,1,0:T(2,128)(2,1)S(1)} async-done(((bf16[128,2,512]{2,1,0:T(2,128)(2,1)}), bf16[128,2,512]{2,1,0:T(2,128)(2,1)S(1)}, u32[]{:S(2)}, u32[]{:S(2)}) %all-to-all-start.2) | async-done | bytes 262176 | tf_op jit(solution)/shard_map/all_to_all | solution.py:156
  118.4 0.8 gather_fusion
  119.2 0.2 fusion.32
  119.5 0.6 stack.2
  120.1 3.3 %all-to-all-start.3 = ((bf16[4,16,512]{2,1,0:T(8,128)(2,1)}), bf16[4,16,512]{2,1,0:T(8,128)(2,1)S(1)}, u32[]{:S(2)}, u32[]{:S(2)}) async-start(bf16[4,16,512]{2,1,0:T(8,128)(2,1)} %stack.2), calls=%async_computation.3 | async-start | bytes 131072 | tf_op jit(solution)/shard_map/all_to_all | solution.py:12
  123.4 0.4 fusion.11
  123.8 0.6 copy.46
  124.4 4.6 %all-to-all-done.3 = bf16[4,16,512]{2,1,0:T(8,128)(2,1)S(1)} async-done(((bf16[4,16,512]{2,1,0:T(8,128)(2,1)}), bf16[4,16,512]{2,1,0:T(8,128)(2,1)S(1)}, u32[]{:S(2)}, u32[]{:S(2)}) %all-to-all-start.3) | async-done | bytes 65568 | tf_op jit(solution)/shard_map/all_to_all | solution.py:12
  129.0 0.6 copy.35
  (53 shorter events, 1.6 us)
Async XLA Ops:
  7.2 60.7 %copy-start = (bf16[1,2048,256]{2,1,0:T(8,128)(2,1)S(1)}, bf16[1,2048,256]{2,1,0:T(8,128)(2,1)}, u32[]{:S(2)}) copy-start(bf16[1,2048,256]{2,1,0:T(8,128)(2,1)} %param.17) | copy-start | bytes 3145732
  7.2 21.1 %copy-start.5 = (bf16[8,2048]{1,0:T(8,128)(2,1)S(1)}, bf16[8,2048]{1,0:T(8,128)(2,1)}, u32[]{:S(2)}) copy-start(bf16[8,2048]{1,0:T(8,128)(2,1)} %param.19) | copy-start | bytes 98308
  7.2 21.1 %copy-start.10 = (s32[8]{0:T(128)S(1)}, s32[8]{0:T(128)}, u32[]{:S(2)}) copy-start(s32[8]{0:T(128)} %param.25) | copy-start | bytes 100
  7.2 21.3 %copy-start.8 = (bf16[8,128]{1,0:T(8,128)(2,1)S(1)}, bf16[8,128]{1,0:T(8,128)(2,1)}, u32[]{:S(2)}) copy-start(bf16[8,128]{1,0:T(8,128)(2,1)} %param.23) | copy-start | bytes 6148
  7.2 21.6 %copy-start.6 = (s32[16,8]{0,1:T(8,128)S(1)}, s32[16,8]{0,1:T(8,128)}, u32[]{:S(2)}) copy-start(s32[16,8]{0,1:T(8,128)} %param.15) | copy-start | bytes 1540
  8.8 34.8 %copy-start.3 = (bf16[2048,128]{1,0:T(8,128)(2,1)S(1)}, bf16[2048,128]{1,0:T(8,128)(2,1)}, u32[]{:S(2)}) copy-start(bf16[2048,128]{1,0:T(8,128)(2,1)} %param.20) | copy-start | bytes 1572868
  8.8 34.8 %copy-start.7 = (f32[1,2048]{1,0:T(1,128)S(1)}, f32[1,2048]{1,0:T(1,128)}, u32[]{:S(2)}) copy-start(f32[1,2048]{1,0:T(1,128)} %param.21) | copy-start | bytes 24580
  10.7 32.1 %all-to-all-start = ((bf16[128,2,512]{2,1,0:T(2,128)(2,1)}), bf16[128,2,512]{2,1,0:T(2,128)(2,1)S(1)}, u32[]{:S(2)}, u32[]{:S(2)}) async-start(bf16[128,2,512]{2,1,0:T(2,128)(2,1)} %reshape.491), calls=%async_computation | async-start | bytes 524288 | tf_op jit(solution)/shard_map/all_to_all | solution.py:142
  28.1 37.8 %all-gather.3.cloned.1.call-start = ((), (), s32[]{:S(2)}) async-start(), calls=%async_computation.4 | async-start | bytes 1310720 | tf_op jit(solution)/shard_map/all_gather | solution.py:143
  42.8 0.7 copy-start.2
  49.6 17.8 %copy-start.1 = (bf16[1,2048,256]{2,1,0:T(8,128)(2,1)S(1)}, bf16[1,2048,256]{2,1,0:T(8,128)(2,1)}, u32[]{:S(2)}) copy-start(bf16[1,2048,256]{2,1,0:T(8,128)(2,1)} %param.16) | copy-start | bytes 3145732
  71.4 16.9 %all-to-all-start.1 = ((bf16[256,4,512]{2,0,1:T(8,128)(2,1)}), bf16[256,4,512]{2,0,1:T(8,128)(2,1)S(1)}, u32[]{:S(2)}, u32[]{:S(2)}) async-start(bf16[256,4,512]{2,0,1:T(8,128)(2,1)} %bitcast.108), calls=%async_computation.1 | async-start | bytes 2097152 | tf_op jit(solution)/shard_map/all_to_all | solution.py:153
  77.0 26.7 %copy-start.9 = (bf16[8,128]{1,0:T(8,128)(2,1)S(1)}, bf16[8,128]{1,0:T(8,128)(2,1)}, u32[]{:S(2)}) copy-start(bf16[8,128]{1,0:T(8,128)(2,1)} %param.24) | copy-start | bytes 6148
  89.4 28.9 %all-to-all-start.2 = ((bf16[128,2,512]{2,1,0:T(2,128)(2,1)}), bf16[128,2,512]{2,1,0:T(2,128)(2,1)S(1)}, u32[]{:S(2)}, u32[]{:S(2)}) async-start(bf16[128,2,512]{2,1,0:T(2,128)(2,1)} %reshape.494), calls=%async_computation.2 | async-start | bytes 524288 | tf_op jit(solution)/shard_map/all_to_all | solution.py:156
  104.0 19.5 %copy-start.4 = (bf16[2048,128]{1,0:T(8,128)(2,1)S(1)}, bf16[2048,128]{1,0:T(8,128)(2,1)}, u32[]{:S(2)}) copy-start(bf16[2048,128]{1,0:T(8,128)(2,1)} %param.22) | copy-start | bytes 1572868
  120.1 8.9 %all-to-all-start.3 = ((bf16[4,16,512]{2,1,0:T(8,128)(2,1)}), bf16[4,16,512]{2,1,0:T(8,128)(2,1)S(1)}, u32[]{:S(2)}, u32[]{:S(2)}) async-start(bf16[4,16,512]{2,1,0:T(8,128)(2,1)} %stack.2), calls=%async_computation.3 | async-start | bytes 131072 | tf_op jit(solution)/shard_map/all_to_all | solution.py:12
Sparse Core Ops, SparseCore 0:
  43.7 22.2 all-gather.2
